TPU v7x, 32 devices: a whole 2x2x4 slice. The times are simulated.
32 devices in a mesh: groups: 2 (over y), pairs: 4 (over z), mp: 4 (over x, core).
Axes of the slice: x: 2, y: 2, z: 4, core: 2. Of those that a mesh axis runs over, the one named last changes fastest.
Arguments:
- tokens: bfloat16 [512, 768], P(('groups', 'pairs'), 'mp'), parts along dimension 0, may hold values from -6 to 6
- pair_list: int32 [16, 2], P(('groups', 'pairs')), parts along dimension 0, may hold values from 0 to 7, as said below
- confidence: float32 [16, 64], P(('groups', 'pairs')), parts along dimension 0, may hold values from 0.1 to 10
- gain_self: float32 [768], replicated, may hold values from 0.1 to 1.9
- gain_query: float32 [768], replicated, may hold values from 0.1 to 1.9
- gain_context: float32 [768], replicated, may hold values from 0.1 to 1.9
- gain_mlp: float32 [768], replicated, may hold values from 0.1 to 1.9
- self_qkv: bfloat16 [3, 768, 768], P(None, None, 'mp'), may hold values from -1 to 1
- self_out: bfloat16 [768, 768], P('mp'), may hold values from -0.21875 to 0.21875
- cross_query: bfloat16 [768, 768], P(None, 'mp'), may hold values from -1 to 1
- cross_kv: bfloat16 [2, 768, 768], P(None, None, 'mp'), may hold values from -1 to 1
- cross_out: bfloat16 [768, 768], P('mp'), may hold values from -0.21875 to 0.21875
- mlp_up: bfloat16 [768, 3072], P(None, 'mp'), may hold values from -0.21875 to 0.21875
- mlp_down: bfloat16 [3072, 768], P('mp'), may hold values from -0.109375 to 0.109375
Outputs:
- image_features: bfloat16 [512, 768], P(('groups', 'pairs'), 'mp'), parts along dimension 0
There are 2 independent parts, one for each index of `groups`. A program takes and returns all parts, laid end to end along the dimension named above; an argument that names none is the same for every part. Nothing has to cross between parts.
Inputs may be any that keep to these rules, and one draw needn't show every extreme that they name: `pair_list`: in each block of 2 consecutive pairs the 4 images named are distinct and have distinct owners, the owner of image i being i // 2; the images of each owner are named in exactly 4 blocks; some images are named by no pair.
All inputs are finite; a program needn't handle non-finite values.
Results may differ from a plain program's by a relative error of at most 0.012.
Values may be sent and summed in bfloat16 or wider, within the bound.
No kernel may reach another device: no remote copies, remote signals or barrier semaphores. Data moves between devices by JAX's collectives and lax.ppermute only.
A program may use at most 64 MiB of HBM per device.

v0:
```python
import jax
import jax.numpy as jnp
from jax import lax
from jax.sharding import PartitionSpec as P

HEAD = 64
TOKS = 32
EPSILON = 1e-06


def layer_norm(values, gain):
    center = values - jnp.mean(values, axis=-1, keepdims=True)
    spread = jnp.mean(center * center, axis=-1, keepdims=True)
    return (center * lax.rsqrt(spread + EPSILON) * gain).astype(jnp.bfloat16)


def attend(query, keys, values, views_n):
    rows_n, width = query.shape
    heads_n = width // HEAD
    qh = query.reshape(views_n, TOKS, heads_n, HEAD)
    kh = keys.reshape(views_n, TOKS, heads_n, HEAD)
    vh = values.reshape(views_n, TOKS, heads_n, HEAD)
    scores = jnp.einsum("vqhc,vkhc->vhqk", qh, kh, preferred_element_type=jnp.float32) * HEAD ** (
        -0.5
    )
    probs = jax.nn.softmax(scores, axis=-1).astype(jnp.bfloat16)
    mixed = jnp.einsum("vhqk,vkhc->vqhc", probs, vh, preferred_element_type=jnp.float32)
    return mixed.astype(jnp.bfloat16).reshape(rows_n, width)


def partner(values):
    shape = values.shape
    paired = values.reshape((shape[0] // 2, 2) + shape[1:])
    return jnp.flip(paired, axis=1).reshape(shape)


def summed_full(term):
    return lax.psum(term.astype(jnp.bfloat16), "mp").astype(jnp.float32)


def per_device(
    tokens,
    pair_list,
    confidence,
    gain_self,
    gain_query,
    gain_context,
    gain_mlp,
    self_qkv,
    self_out,
    cross_query,
    cross_kv,
    cross_out,
    mlp_up,
    mlp_down,
):
    quarter = tokens.shape[1]
    img_dev = tokens.shape[0] // TOKS
    pair_dev = pair_list.shape[0]
    views_n = 2 * pair_dev
    owners_n = lax.axis_size("pairs")
    own = lax.axis_index("pairs")
    table = lax.all_gather(pair_list, "pairs", axis=0, tiled=True).reshape(owners_n, views_n)
    wanted = jnp.where(table // img_dev == own, table % img_dev, -1)
    chosen = jnp.max(wanted, axis=1)
    images = tokens.reshape(img_dev, TOKS, quarter)
    picked = jnp.take(images, jnp.maximum(chosen, 0), axis=0)
    outgoing = jnp.where((chosen >= 0)[:, None, None], picked, jnp.zeros_like(picked))
    arrived = lax.all_to_all(outgoing, "pairs", split_axis=0, concat_axis=0, tiled=True)
    source = pair_list.reshape(views_n) // img_dev
    slices = jnp.take(arrived, source, axis=0)
    start = lax.all_gather(slices, "mp", axis=2, tiled=True)
    width = start.shape[2]
    rows_n = views_n * TOKS
    begin = start.astype(jnp.float32).reshape(rows_n, width)
    context = layer_norm(partner(start.astype(jnp.float32)), gain_context).reshape(rows_n, width)
    offset = lax.axis_index("mp") * quarter
    normed = layer_norm(begin, gain_self)
    qkv = jnp.einsum("rd,kdc->krc", normed, self_qkv, preferred_element_type=jnp.float32).astype(
        jnp.bfloat16
    )
    term = jnp.dot(
        attend(qkv[0], qkv[1], qkv[2], views_n), self_out, preferred_element_type=jnp.float32
    )
    resid = begin + summed_full(term)
    normed = layer_norm(resid, gain_query)
    query = jnp.dot(normed, cross_query, preferred_element_type=jnp.float32).astype(jnp.bfloat16)
    keyval = jnp.einsum(
        "rd,kdc->krc", context, cross_kv, preferred_element_type=jnp.float32
    ).astype(jnp.bfloat16)
    term = jnp.dot(
        attend(query, keyval[0], keyval[1], views_n), cross_out, preferred_element_type=jnp.float32
    )
    resid = resid + summed_full(term)
    normed = layer_norm(resid, gain_mlp)
    hidden = jax.nn.gelu(
        jnp.dot(normed, mlp_up, preferred_element_type=jnp.float32), approximate=False
    )
    term = jnp.dot(hidden.astype(jnp.bfloat16), mlp_down, preferred_element_type=jnp.float32)
    resid = resid + summed_full(term)
    final = lax.dynamic_slice_in_dim(resid, offset, quarter, 1)
    conf = confidence.reshape(views_n, TOKS)
    weighted = (final.reshape(views_n, TOKS, quarter) * conf[:, :, None]).reshape(
        views_n, TOKS * quarter
    )
    route = (source[None, :] == jnp.arange(owners_n)[:, None]).astype(jnp.float32)
    back = jnp.dot(route, weighted, precision=lax.Precision.HIGHEST).astype(jnp.bfloat16)
    back_weight = jnp.dot(route, conf, precision=lax.Precision.HIGHEST).astype(jnp.bfloat16)
    got_feat, got_weight = (
        lax.all_to_all(
            back.reshape(owners_n, TOKS, quarter), "pairs", split_axis=0, concat_axis=0, tiled=True
        ),
        lax.all_to_all(back_weight, "pairs", split_axis=0, concat_axis=0, tiled=True),
    )
    owner_match = chosen[None, :] == jnp.arange(img_dev)[:, None]
    numer = jnp.einsum(
        "ij,jtc->itc",
        owner_match.astype(jnp.bfloat16),
        got_feat,
        preferred_element_type=jnp.float32,
    )
    denom = jnp.dot(
        owner_match.astype(jnp.float32),
        got_weight.astype(jnp.float32),
        precision=lax.Precision.HIGHEST,
    )
    result = numer / jnp.maximum(denom, 1.0)[:, :, None]
    return result.astype(jnp.bfloat16).reshape(img_dev * TOKS, quarter)


def solution(mesh):
    return jax.shard_map(
        per_device,
        mesh=mesh,
        in_specs=(
            P(("groups", "pairs"), "mp"),
            P(("groups", "pairs"), None),
            P(("groups", "pairs"), None),
            P(),
            P(),
            P(),
            P(),
            P(None, None, "mp"),
            P("mp", None),
            P(None, "mp"),
            P(None, None, "mp"),
            P("mp", None),
            P(None, "mp"),
            P("mp", None),
        ),
        out_specs=P(("groups", "pairs"), "mp"),
        check_vma=False,
    )
```

profile of v0, /device:TPU:0, one launch (start us, length us, event | category | flops | bytes accessed | tf_op | source)
XLA Modules:
  0.0 180.7 jit_solution(869110114710449456)
XLA Ops:
  6.5 13.0 %all-gather = s32[4,2,2]{2,1,0:T(2,128)S(1)} all-gather(s32[1,2,2]{2,1,0:T(2,128)} %bitcast.90), channel_id=1, replica_groups=mesh['groups'=2,'pairs'=4,'mp'=4] {'pairs'}, dimensions={0}, use_global_device_ids=true | all-gather | bytes 80 | tf_op jit(solution)/shard_map/all_gather | solution.py:63
  19.7 0.1 reduce_max.36
  19.9 0.5 copy-done.11
  20.4 1.3 gather_fusion
  21.7 0.7 select_select_fusion
  22.4 3.3 %all-to-all-start = ((bf16[4,32,192]{2,1,0:T(8,128)(2,1)}), bf16[4,32,192]{2,1,0:T(8,128)(2,1)S(1)}, u32[]{:S(2)}, u32[]{:S(2)}) async-start(bf16[4,32,192]{2,1,0:T(8,128)(2,1)} %select_select_fusion), calls=%async_computation | async-start | bytes 131072 | tf_op jit(solution)/shard_map/all_to_all | solution.py:69
  25.7 0.8 reshape.277
  26.5 0.8 reshape.275
  27.3 0.5 compare_and_fusion
  27.8 3.6 %all-to-all-done = bf16[4,32,192]{2,1,0:T(8,128)(2,1)S(1)} async-done(((bf16[4,32,192]{2,1,0:T(8,128)(2,1)}), bf16[4,32,192]{2,1,0:T(8,128)(2,1)S(1)}, u32[]{:S(2)}, u32[]{:S(2)}) %all-to-all-start) | async-done | bytes 49184 | tf_op jit(solution)/shard_map/all_to_all | solution.py:69
  31.4 0.5 gather_fusion.1
  32.0 0.2 copy.73
  32.2 8.6 %all_gather.7 = bf16[4,32,768]{1,0,2:T(4,128)(2,1)S(1)} all-gather(bf16[4,32,192]{1,0,2:T(4,128)(2,1)S(1)} %copy.73), channel_id=1, replica_groups=mesh['groups'=2,'pairs'=4,'mp'=4] {'mp'}, dimensions={2}, use_global_device_ids=true | all-gather | bytes 245760 | tf_op jit(solution)/shard_map/all_gather | solution.py:72
  40.8 0.8 convert_reduce_fusion
  41.6 0.4 copy.74
  42.1 0.8 multiply_reduce_fusion.1
  42.9 0.7 div.88
  43.6 1.3 convert_element_type.84
  44.9 7.5 %rev.4 = f32[2,2,32,768]{2,1,0,3:T(2,128)S(1)} reverse(f32[2,2,32,768]{2,1,0,3:T(2,128)} %bitcast.83), dimensions={1} | reverse | bytes 786432 | tf_op jit(solution)/shard_map/jit(_flip)/rev | solution.py:34
  52.4 0.8 reduce_sum.93
  53.2 1.1 multiply_reduce_fusion
  54.4 0.6 copy.83
  55.2 0.8 fusion.18
  56.0 1.6 fusion.122
  57.6 0.1 reshape.312
  57.7 0.1 reshape.313
  57.9 0.2 convolution_multiply_fusion.1
  58.2 0.1 reshape.311
  58.4 0.3 fusion.6
  58.6 0.1 copy.82
  58.7 0.1 reshape.279
  58.9 0.9 convolution_convert_fusion.3
  59.9 0.1 fusion.15
  60.1 0.3 fusion.123
  60.5 0.1 reshape.316
  60.6 0.1 reshape.314
  60.7 28.6 %all-reduce.4.cloned.1.call-done = bf16[128,768]{1,0:T(8,128)(2,1)} async-done(((bf16[128,768]{1,0:T(8,128)(2,1)}), bf16[128,768]{1,0:T(8,128)(2,1)}) %all-reduce.4.cloned.1.call-update) | async-done | bytes 196624 | tf_op jit(solution)/shard_map/psum | solution.py:38
  89.3 1.0 fusion.77
  90.4 1.1 multiply_reduce_fusion.3
  91.5 0.3 convolution_convert_fusion.6
  91.8 0.1 reshape.315
  92.0 0.2 convolution_multiply_fusion
  92.3 0.3 fusion.7
  92.7 0.1 reshape.283
  92.8 0.9 convolution_convert_fusion.2
  93.9 31.7 %all-reduce.6.cloned.1.call-done = bf16[128,768]{1,0:T(8,128)(2,1)} async-done(((bf16[128,768]{1,0:T(8,128)(2,1)}), bf16[128,768]{1,0:T(8,128)(2,1)}) %all-reduce.6.cloned.1.call-update) | async-done | bytes 196624 | tf_op jit(solution)/shard_map/psum | solution.py:38
  125.6 1.1 fusion.117
  126.7 0.2 multiply_reduce_fusion.2
  126.9 2.1 %convolution_convert_fusion.1 = bf16[128,768]{1,0:T(8,128)(2,1)} fusion(bf16[768,768]{1,0:T(8,128)(2,1)S(1)} %copy-done, bf16[768,768]{1,0:T(8,128)(2,1)S(1)} %copy-done.13, f32[128,768]{1,0:T(8,128)S(1)} %get-tuple-element.6, f32[768]{0:T(1024)S(1)} %copy-done.14, f32[128]{0:T(128)S(1)} %add_rsqrt_fusion.2, f32[128]{0:T(128)S(1)} %broadcast_multiply_fusion.2), kind=kOutput, calls=%fused_computation.9 | convolution fusion | flops 308871168 | bytes 2953216 | tf_op jit(solution)/shard_map/dot_general | solution.py:99
  129.1 0.1 fusion.9
  129.2 0.6 copy.94
  129.8 4.6 %all-to-all-start.2 = ((bf16[4,1,32]{2,1,0:T(2,128)(2,1)}), bf16[4,1,32]{2,1,0:T(2,128)(2,1)S(1)}, u32[]{:S(2)}, u32[]{:S(2)}) async-start(bf16[4,1,32]{2,1,0:T(2,128)(2,1)} %copy.94), calls=%async_computation.2 | async-start | bytes 4096 | tf_op jit(solution)/shard_map/all_to_all | solution.py:113
  134.5 0.1 mul.147
  134.6 26.3 %all-reduce.8.cloned.1.call-done = bf16[128,768]{1,0:T(8,128)(2,1)} async-done(((bf16[128,768]{1,0:T(8,128)(2,1)}), bf16[128,768]{1,0:T(8,128)(2,1)}) %all-reduce.8.cloned.1.call-update) | async-done | bytes 196624 | tf_op jit(solution)/shard_map/psum | solution.py:38
  160.9 1.0 dynamic-slice_add_fusion
  161.9 0.1 reshape.284
  162.1 0.2 convolution_convert_fusion
  162.3 0.7 reshape.285
  163.0 4.6 %all-to-all-start.1 = ((bf16[4,32,192]{2,1,0:T(8,128)(2,1)}), bf16[4,32,192]{2,1,0:T(8,128)(2,1)S(1)}, u32[]{:S(2)}, u32[]{:S(2)}) async-start(bf16[4,32,192]{2,1,0:T(8,128)(2,1)} %reshape.285), calls=%async_computation.1 | async-start | bytes 131072 | tf_op jit(solution)/shard_map/all_to_all | solution.py:110
  167.6 0.1 convolution_maximum_fusion
  167.7 0.1 copy.95
  167.8 5.5 %all-to-all-done.1 = bf16[4,32,192]{2,1,0:T(8,128)(2,1)S(1)} async-done(((bf16[4,32,192]{2,1,0:T(8,128)(2,1)}), bf16[4,32,192]{2,1,0:T(8,128)(2,1)S(1)}, u32[]{:S(2)}, u32[]{:S(2)}) %all-to-all-start.1) | async-done | bytes 49184 | tf_op jit(solution)/shard_map/all_to_all | solution.py:110
  173.4 0.2 fusion.8
  173.5 0.6 copy.96
  (65 shorter events, 1.3 us)
Async XLA Ops:
  6.5 120.3 %copy-start = (bf16[768,768]{1,0:T(8,128)(2,1)S(1)}, bf16[768,768]{1,0:T(8,128)(2,1)}, u32[]{:S(2)}) copy-start(bf16[768,768]{1,0:T(8,128)(2,1)} %param.27) | copy-start | bytes 3538948
  19.8 0.5 copy-start.11
  22.4 9.0 %all-to-all-start = ((bf16[4,32,192]{2,1,0:T(8,128)(2,1)}), bf16[4,32,192]{2,1,0:T(8,128)(2,1)S(1)}, u32[]{:S(2)}, u32[]{:S(2)}) async-start(bf16[4,32,192]{2,1,0:T(8,128)(2,1)} %select_select_fusion), calls=%async_computation | async-start | bytes 131072 | tf_op jit(solution)/shard_map/all_to_all | solution.py:69
  25.7 63.6 %all-reduce.4.cloned.1.call-start = ((), (), s32[]{:S(2)}) async-start(), calls=%async_computation.3 | async-start | bytes 393216 | tf_op jit(solution)/shard_map/psum | solution.py:38
  53.2 1.9 %copy-start.6 = (f32[768]{0:T(1024)S(1)}, f32[768]{0:T(1024)}, u32[]{:S(2)}) copy-start(f32[768]{0:T(1024)} %param.17) | copy-start | bytes 9220
  57.6 1.3 copy-start.3
  57.9 2.0 %copy-start.7 = (f32[768]{0:T(1024)S(1)}, f32[768]{0:T(1024)}, u32[]{:S(2)}) copy-start(f32[768]{0:T(1024)} %param.19) | copy-start | bytes 9220
  58.2 1.9 %copy-start.2 = (bf16[2,768,192]{1,2,0:T(8,128)(2,1)S(1)}, bf16[2,768,192]{1,2,0:T(8,128)(2,1)}, u32[]{:S(2)}) copy-start(bf16[2,768,192]{1,2,0:T(8,128)(2,1)} %param.24) | copy-start | bytes 1769476
  59.8 65.8 %all-reduce.6.cloned.1.call-start = ((), (), s32[]{:S(2)}) async-start(), calls=%async_computation.4 | async-start | bytes 393216 | tf_op jit(solution)/shard_map/psum | solution.py:38
  60.1 31.4 %copy-start.4 = (bf16[768,192]{0,1:T(8,128)(2,1)S(1)}, bf16[768,192]{0,1:T(8,128)(2,1)}, u32[]{:S(2)}) copy-start(bf16[768,192]{0,1:T(8,128)(2,1)} %param.23) | copy-start | bytes 884740
  60.1 31.4 %copy-start.8 = (f32[768]{0:T(1024)S(1)}, f32[768]{0:T(1024)}, u32[]{:S(2)}) copy-start(f32[768]{0:T(1024)} %param.18) | copy-start | bytes 9220
  91.5 1.3 copy-start.5
  92.0 1.8 copy-start.9
  92.0 33.6 %copy-start.1 = (bf16[128,768]{1,0:T(8,128)(2,1)S(1)}, bf16[128,768]{1,0:T(8,128)(2,1)}, u32[]{:S(2)}) copy-start(bf16[128,768]{1,0:T(8,128)(2,1)} %all-reduce.4.cloned.1.call-done) | copy-start | bytes 589828
  92.6 34.3 %copy-start.14 = (f32[768]{0:T(1024)S(1)}, f32[768]{0:T(1024)}, u32[]{:S(2)}) copy-start(f32[768]{0:T(1024)} %param.20) | copy-start | bytes 9220
  93.7 67.2 %all-reduce.8.cloned.1.call-start = ((), (), s32[]{:S(2)}) async-start(), calls=%async_computation.5 | async-start | bytes 393216 | tf_op jit(solution)/shard_map/psum | solution.py:38
  93.9 33.0 %copy-start.13 = (bf16[768,768]{1,0:T(8,128)(2,1)S(1)}, bf16[768,768]{1,0:T(8,128)(2,1)}, u32[]{:S(2)}) copy-start(bf16[768,768]{1,0:T(8,128)(2,1)} %param.26) | copy-start | bytes 3538948
  126.9 2.2 %copy-start.10 = (s32[4]{0:T(128)S(1)}, s32[4]{0:T(128)}, u32[]{:S(2)}) copy-start(s32[4]{0:T(128)} %get-tuple-element.8) | copy-start | bytes 52
  129.1 38.6 %copy-start.12 = (s32[4]{0:T(128)S(1)}, s32[4]{0:T(128)}, u32[]{:S(2)}) copy-start(s32[4]{0:T(128)} %copy-done.11) | copy-start | bytes 52
  129.8 33.2 %all-to-all-start.2 = ((bf16[4,1,32]{2,1,0:T(2,128)(2,1)}), bf16[4,1,32]{2,1,0:T(2,128)(2,1)S(1)}, u32[]{:S(2)}, u32[]{:S(2)}) async-start(bf16[4,1,32]{2,1,0:T(2,128)(2,1)} %copy.94), calls=%async_computation.2 | async-start | bytes 4096 | tf_op jit(solution)/shard_map/all_to_all | solution.py:113
  163.0 10.3 %all-to-all-start.1 = ((bf16[4,32,192]{2,1,0:T(8,128)(2,1)}), bf16[4,32,192]{2,1,0:T(8,128)(2,1)S(1)}, u32[]{:S(2)}, u32[]{:S(2)}) async-start(bf16[4,32,192]{2,1,0:T(8,128)(2,1)} %reshape.285), calls=%async_computation.1 | async-start | bytes 131072 | tf_op jit(solution)/shard_map/all_to_all | solution.py:110
Sparse Core Ops, SparseCore 0:
  59.9 29.3 all-reduce.3
  93.8 31.7 all-reduce.5
  129.2 31.6 all-reduce.7
where the time goes:
time: 181 us
  waiting for transfers between devices  95.8 us (53%)
  blocking collectives  21.6 us (12%)
  local copies, waits for them, and re-layouts  17.5 us (10%)
  between operations  13.6 us (8%)
  starting transfers between devices  12.6 us (7%)
  other arithmetic  12 us (7%)
  matrix products  7.72 us (4%)
    psum x3, waiting for transfers between devices, summed_full(): return lax.psum(term.astype(jnp.bfloat16), 'mp').astype(jnp.float32)  86.6 us
    all_gather x1, blocking collectives, per_device(): lax.all_gather(pair_list, 'pairs', axis=0, tiled=True)  13 us
    all_gather x1, blocking collectives, per_device(): start = lax.all_gather(slices, 'mp', axis=2, tiled=True)  8.6 us
    rev x2, local copies, waits for them, and re-layouts, partner(): return jnp.flip(paired, axis=1).reshape(shape)  8.14 us
    all_to_all x1, waiting for transfers between devices, per_device(): lax.all_to_all(back.reshape(owners_n, TOKS, quarter), 'pairs', split_axis...  5.53 us
    all_to_all x1, starting transfers between devices, per_device(): lax.all_to_all(back_weight, 'pairs', split_axis=0, concat_axis=0, tiled=T...  4.6 us
    all_to_all x1, starting transfers between devices, per_device(): lax.all_to_all(back.reshape(owners_n, TOKS, quarter), 'pairs', split_axis...  4.6 us
    reduce_sum x4, other arithmetic, layer_norm(): center = values - jnp.mean(values, axis=-1, keepdims=True)  3.78 us
  transfers between devices with their start and end apart: 6, of which 5 were waited for; matrix products, arithmetic and copies ran while one was open for 3% of the time, Pallas kernels for 0%

commit v1 on v0

--- a/solution.py
+++ b/solution.py
@@ -6,6 +6,16 @@
 HEAD = 64
 TOKS = 32
 EPSILON = 1e-06
+
+
+def pass_along(block, axis, along):
+    n_dev = lax.axis_size(axis)
+    held, pieces = (block, [block])
+    for _ in range(n_dev - 1):
+        held = lax.ppermute(held, axis, [(i, (i + 1) % n_dev) for i in range(n_dev)])
+        pieces.insert(0, held)
+    line = jnp.concatenate(pieces, axis=along)
+    return jnp.roll(line, (lax.axis_index(axis) + 1) * block.shape[along], axis=along)
 
 
 def layer_norm(values, gain):
@@ -69,7 +79,7 @@
     arrived = lax.all_to_all(outgoing, "pairs", split_axis=0, concat_axis=0, tiled=True)
     source = pair_list.reshape(views_n) // img_dev
     slices = jnp.take(arrived, source, axis=0)
-    start = lax.all_gather(slices, "mp", axis=2, tiled=True)
+    start = pass_along(slices, "mp", 2)
     width = start.shape[2]
     rows_n = views_n * TOKS
     begin = start.astype(jnp.float32).reshape(rows_n, width)

time: 181 us -> 173 us (0.956)
  waiting for transfers between devices: 95.8 us -> 109 us
  local copies, waits for them, and re-layouts: 17.5 us -> 8.31 us
  blocking collectives: 21.6 us -> 13 us
  other arithmetic: 12 us -> 8.13 us
    ppermute x0 -> x3, waiting for transfers between devices: none -> 11.1 us  [pass_along(): lax.ppermute(held, axis, [(i, (i + 1) % n_dev) for i in range(n_dev)])]
    all_gather x1 -> x0, blocking collectives: 8.6 us -> none  [per_device(): start = lax.all_gather(slices, 'mp', axis=2, tiled=True)]
    rev x2 -> x1, local copies, waits for them, and re-layouts: 8.14 us -> 0.03 us  [partner(): return jnp.flip(paired, axis=1).reshape(shape)]
  transfers between devices with their start and end apart: 6 -> 9, of which waited for: 5 -> 8; matrix products, arithmetic and copies ran while one was open for 3% -> 3% of each run, Pallas kernels for 0% -> 0%
where the time goes in v1:
time: 173 us; the launch traced here: 172 us
  waiting for transfers between devices  109 us (63%)
  between operations  13.6 us (8%)
  blocking collectives  13 us (8%)
  starting transfers between devices  12.6 us (7%)
  local copies, waits for them, and re-layouts  8.31 us (5%)
  other arithmetic  8.13 us (5%)
  matrix products  7.72 us (4%)
    psum x3, waiting for transfers between devices, summed_full(): return lax.psum(term.astype(jnp.bfloat16), 'mp').astype(jnp.float32)  88.1 us
    all_gather x1, blocking collectives, per_device(): lax.all_gather(pair_list, 'pairs', axis=0, tiled=True)  13 us
    ppermute x3, waiting for transfers between devices, pass_along(): lax.ppermute(held, axis, [(i, (i + 1) % n_dev) for i in range(n_dev)])  11.1 us
    all_to_all x1, waiting for transfers between devices, per_device(): lax.all_to_all(back.reshape(owners_n, TOKS, quarter), 'pairs', split_axis...  5.53 us
    all_to_all x1, starting transfers between devices, per_device(): lax.all_to_all(back.reshape(owners_n, TOKS, quarter), 'pairs', split_axis...  4.6 us
    all_to_all x1, starting transfers between devices, per_device(): lax.all_to_all(back_weight, 'pairs', split_axis=0, concat_axis=0, tiled=T...  4.6 us
    all_to_all x1, waiting for transfers between devices, per_device(): lax.all_to_all(outgoing, 'pairs', split_axis=0, concat_axis=0, tiled=True)  4.1 us
  transfers between devices with their start and end apart: 9, of which 8 were waited for; matrix products, arithmetic and copies ran while one was open for 3% of the time, Pallas kernels for 0%

profile of v1, /device:TPU:0, one launch (start us, length us, event | category | flops | bytes accessed | tf_op | source)
XLA Modules:
  0.0 172.2 jit_solution(10626616977184623155)
XLA Ops:
  6.5 13.0 %all-gather = s32[4,2,2]{2,1,0:T(2,128)S(1)} all-gather(s32[1,2,2]{2,1,0:T(2,128)} %bitcast.95), channel_id=1, replica_groups=mesh['groups'=2,'pairs'=4,'mp'=4] {'pairs'}, dimensions={0}, use_global_device_ids=true | all-gather | bytes 80 | tf_op jit(solution)/shard_map/all_gather | solution.py:73
  19.7 0.1 reduce_max.36
  19.9 1.3 gather_fusion
  21.2 0.7 select_select_fusion
  21.9 3.3 %all-to-all-start = ((bf16[4,32,192]{2,1,0:T(8,128)(2,1)}), bf16[4,32,192]{2,1,0:T(8,128)(2,1)S(1)}, u32[]{:S(2)}, u32[]{:S(2)}) async-start(bf16[4,32,192]{2,1,0:T(8,128)(2,1)} %select_select_fusion), calls=%async_computation | async-start | bytes 131072 | tf_op jit(solution)/shard_map/all_to_all | solution.py:79
  25.2 0.8 reshape.277
  26.0 0.8 reshape.275
  26.8 4.1 %all-to-all-done = bf16[4,32,192]{2,1,0:T(8,128)(2,1)S(1)} async-done(((bf16[4,32,192]{2,1,0:T(8,128)(2,1)}), bf16[4,32,192]{2,1,0:T(8,128)(2,1)S(1)}, u32[]{:S(2)}, u32[]{:S(2)}) %all-to-all-start) | async-done | bytes 49184 | tf_op jit(solution)/shard_map/all_to_all | solution.py:79
  30.9 0.5 gather_fusion.1
  31.5 3.7 %collective-permute-done = bf16[4,32,192]{2,1,0:T(8,128)(2,1)S(1)} collective-permute-done((bf16[4,32,192]{2,1,0:T(8,128)(2,1)S(1)}, bf16[4,32,192]{2,1,0:T(8,128)(2,1)S(1)}, u32[]{:S(2)}, u32[]{:S(2)}) %collective-permute-start) | collective-permute-done | bytes 49184 | tf_op jit(solution)/shard_map/ppermute | solution.py:15
  35.2 3.7 %collective-permute-done.1 = bf16[4,32,192]{2,1,0:T(8,128)(2,1)S(1)} collective-permute-done((bf16[4,32,192]{2,1,0:T(8,128)(2,1)S(1)}, bf16[4,32,192]{2,1,0:T(8,128)(2,1)S(1)}, u32[]{:S(2)}, u32[]{:S(2)}) %collective-permute-start.1) | collective-permute-done | bytes 49184 | tf_op jit(solution)/shard_map/ppermute | solution.py:15
  38.9 3.7 %collective-permute-done.2 = bf16[4,32,192]{2,1,0:T(8,128)(2,1)S(1)} collective-permute-done((bf16[4,32,192]{2,1,0:T(8,128)(2,1)S(1)}, bf16[4,32,192]{2,1,0:T(8,128)(2,1)S(1)}, u32[]{:S(2)}, u32[]{:S(2)}) %collective-permute-start.2) | collective-permute-done | bytes 49184 | tf_op jit(solution)/shard_map/ppermute | solution.py:15
  42.6 0.2 concatenate.6
  42.8 0.1 dynamic-slice_convert_fusion
  43.0 0.1 reverse_reduce_fusion
  43.1 0.2 multiply_reduce_fusion.2
  43.4 0.2 convert_reduce_fusion
  43.6 0.2 multiply_reduce_fusion.3
  44.0 0.1 fusion.15
  44.2 0.3 fusion.120
  44.6 0.2 fusion.18
  44.8 0.3 copy-done.2
  45.1 0.4 fusion.119
  45.5 0.1 reshape.311
  45.6 0.1 reshape.313
  45.8 0.1 reshape.312
  45.9 0.2 convolution_multiply_fusion.1
  46.2 0.3 fusion.6
  46.5 0.1 copy.78
  46.6 0.1 reshape.279
  46.8 0.1 copy-done.4
  46.9 0.9 convolution_convert_fusion.3
  47.9 0.1 reshape.314
  48.0 0.1 reshape.316
  48.1 30.1 %all-reduce.4.cloned.1.call-done = bf16[128,768]{1,0:T(8,128)(2,1)} async-done(((bf16[128,768]{1,0:T(8,128)(2,1)}), bf16[128,768]{1,0:T(8,128)(2,1)}) %all-reduce.4.cloned.1.call-update) | async-done | bytes 196624 | tf_op jit(solution)/shard_map/psum | solution.py:48
  78.2 1.1 fusion.26
  79.3 1.2 multiply_reduce_fusion.1
  80.5 1.1 multiply_convert_fusion.1
  81.7 0.2 convolution_convert_fusion.6
  81.9 0.1 reshape.315
  82.1 0.2 convolution_multiply_fusion
  82.4 0.3 fusion.7
  82.8 0.1 reshape.283
  82.9 0.1 copy-done.6
  83.0 0.9 convolution_convert_fusion.2
  84.1 31.7 %all-reduce.6.cloned.1.call-done = bf16[128,768]{1,0:T(8,128)(2,1)} async-done(((bf16[128,768]{1,0:T(8,128)(2,1)}), bf16[128,768]{1,0:T(8,128)(2,1)}) %all-reduce.6.cloned.1.call-update) | async-done | bytes 196624 | tf_op jit(solution)/shard_map/psum | solution.py:48
  115.8 1.1 fusion.114
  117.0 0.2 multiply_reduce_fusion
  117.2 3.4 %convolution_convert_fusion.1 = bf16[128,768]{1,0:T(8,128)(2,1)} fusion(bf16[768,768]{1,0:T(8,128)(2,1)S(1)} %copy-done, bf16[768,768]{1,0:T(8,128)(2,1)} %param.26, f32[128,768]{1,0:T(8,128)S(1)} %get-tuple-element.6, f32[768]{0:T(1024)S(1)} %copy-done.11, f32[128]{0:T(128)S(1)} %add_rsqrt_fusion.2, f32[128]{0:T(128)S(1)} %broadcast_multiply_fusion.2), kind=kOutput, calls=%fused_computation.7 | convolution fusion | flops 308871168 | bytes 2953216 | tf_op jit(solution)/shard_map/dot_general | solution.py:109
  120.6 0.1 fusion.9
  120.7 0.6 copy.89
  121.3 4.6 %all-to-all-start.2 = ((bf16[4,1,32]{2,1,0:T(2,128)(2,1)}), bf16[4,1,32]{2,1,0:T(2,128)(2,1)S(1)}, u32[]{:S(2)}, u32[]{:S(2)}) async-start(bf16[4,1,32]{2,1,0:T(2,128)(2,1)} %copy.89), calls=%async_computation.2 | async-start | bytes 4096 | tf_op jit(solution)/shard_map/all_to_all | solution.py:123
  126.0 0.1 mul.151
  126.1 26.3 %all-reduce.8.cloned.1.call-done = bf16[128,768]{1,0:T(8,128)(2,1)} async-done(((bf16[128,768]{1,0:T(8,128)(2,1)}), bf16[128,768]{1,0:T(8,128)(2,1)}) %all-reduce.8.cloned.1.call-update) | async-done | bytes 196624 | tf_op jit(solution)/shard_map/psum | solution.py:48
  152.5 1.0 dynamic-slice_add_fusion
  153.5 0.1 reshape.284
  153.6 0.2 convolution_convert_fusion
  153.8 0.7 reshape.285
  154.6 4.6 %all-to-all-start.1 = ((bf16[4,32,192]{2,1,0:T(8,128)(2,1)}), bf16[4,32,192]{2,1,0:T(8,128)(2,1)S(1)}, u32[]{:S(2)}, u32[]{:S(2)}) async-start(bf16[4,32,192]{2,1,0:T(8,128)(2,1)} %reshape.285), calls=%async_computation.1 | async-start | bytes 131072 | tf_op jit(solution)/shard_map/all_to_all | solution.py:120
  159.2 0.1 convolution_maximum_fusion
  159.3 0.1 copy.90
  159.4 5.5 %all-to-all-done.1 = bf16[4,32,192]{2,1,0:T(8,128)(2,1)S(1)} async-done(((bf16[4,32,192]{2,1,0:T(8,128)(2,1)}), bf16[4,32,192]{2,1,0:T(8,128)(2,1)S(1)}, u32[]{:S(2)}, u32[]{:S(2)}) %all-to-all-start.1) | async-done | bytes 49184 | tf_op jit(solution)/shard_map/all_to_all | solution.py:120
  164.9 0.2 fusion.8
  165.1 0.6 copy.91
  (63 shorter events, 1.4 us)
Async XLA Ops:
  6.5 110.6 %copy-start = (bf16[768,768]{1,0:T(8,128)(2,1)S(1)}, bf16[768,768]{1,0:T(8,128)(2,1)}, u32[]{:S(2)}) copy-start(bf16[768,768]{1,0:T(8,128)(2,1)} %param.27) | copy-start | bytes 3538948
  21.9 9.0 %all-to-all-start = ((bf16[4,32,192]{2,1,0:T(8,128)(2,1)}), bf16[4,32,192]{2,1,0:T(8,128)(2,1)S(1)}, u32[]{:S(2)}, u32[]{:S(2)}) async-start(bf16[4,32,192]{2,1,0:T(8,128)(2,1)} %select_select_fusion), calls=%async_computation | async-start | bytes 131072 | tf_op jit(solution)/shard_map/all_to_all | solution.py:79
  25.2 53.0 %all-reduce.4.cloned.1.call-start = ((), (), s32[]{:S(2)}) async-start(), calls=%async_computation.3 | async-start | bytes 393216 | tf_op jit(solution)/shard_map/psum | solution.py:48
  31.5 3.7 %collective-permute-start = (bf16[4,32,192]{2,1,0:T(8,128)(2,1)S(1)}, bf16[4,32,192]{2,1,0:T(8,128)(2,1)S(1)}, u32[]{:S(2)}, u32[]{:S(2)}) collective-permute-start(bf16[4,32,192]{2,1,0:T(8,128)(2,1)S(1)} %broadcast_select_fusion), channel_id=1, source_target_pairs={{0,1},{1,2},{2,3},{3,0},{4,5},{5,6},{6,7},{7,4},{8,9},{9,10},{10,1... | collective-permute-start | bytes 147464 | tf_op jit(solution)/shard_map/ppermute | solution.py:15
  35.2 3.7 %collective-permute-start.1 = (bf16[4,32,192]{2,1,0:T(8,128)(2,1)S(1)}, bf16[4,32,192]{2,1,0:T(8,128)(2,1)S(1)}, u32[]{:S(2)}, u32[]{:S(2)}) collective-permute-start(bf16[4,32,192]{2,1,0:T(8,128)(2,1)S(1)} %collective-permute-done), channel_id=1, source_target_pairs={{0,1},{1,2},{2,3},{3,0},{4,5},{5,6},{6,7},{7,4},{8,9},{9,10},{10,1... | collective-permute-start | bytes 147464 | tf_op jit(solution)/shard_map/ppermute | solution.py:15
  38.9 3.7 %collective-permute-start.2 = (bf16[4,32,192]{2,1,0:T(8,128)(2,1)S(1)}, bf16[4,32,192]{2,1,0:T(8,128)(2,1)S(1)}, u32[]{:S(2)}, u32[]{:S(2)}) collective-permute-start(bf16[4,32,192]{2,1,0:T(8,128)(2,1)S(1)} %collective-permute-done.1), channel_id=1, source_target_pairs={{0,1},{1,2},{2,3},{3,0},{4,5},{5,6},{6,7},{7,4},{8,9},{9,10},{10,1... | collective-permute-start | bytes 147464 | tf_op jit(solution)/shard_map/ppermute | solution.py:15
  42.8 1.3 copy-start.7
  42.9 1.2 copy-start.3
  43.3 1.3 copy-start.8
  43.9 1.2 copy-start.2
  45.9 1.0 copy-start.4
  46.6 33.9 %copy-start.9 = (f32[768]{0:T(1024)S(1)}, f32[768]{0:T(1024)}, u32[]{:S(2)}) copy-start(f32[768]{0:T(1024)} %param.18) | copy-start | bytes 9220
  47.8 33.9 %copy-start.5 = (bf16[768,192]{0,1:T(8,128)(2,1)S(1)}, bf16[768,192]{0,1:T(8,128)(2,1)}, u32[]{:S(2)}) copy-start(bf16[768,192]{0,1:T(8,128)(2,1)} %param.23) | copy-start | bytes 884740
  47.8 68.0 %all-reduce.6.cloned.1.call-start = ((), (), s32[]{:S(2)}) async-start(), calls=%async_computation.4 | async-start | bytes 393216 | tf_op jit(solution)/shard_map/psum | solution.py:48
  82.1 1.0 copy-start.6
  82.4 1.6 copy-start.10
  82.4 33.4 %copy-start.1 = (bf16[128,768]{1,0:T(8,128)(2,1)S(1)}, bf16[128,768]{1,0:T(8,128)(2,1)}, u32[]{:S(2)}) copy-start(bf16[128,768]{1,0:T(8,128)(2,1)} %all-reduce.4.cloned.1.call-done) | copy-start | bytes 589828
  82.8 34.4 %copy-start.11 = (f32[768]{0:T(1024)S(1)}, f32[768]{0:T(1024)}, u32[]{:S(2)}) copy-start(f32[768]{0:T(1024)} %param.20) | copy-start | bytes 9220
  83.9 68.5 %all-reduce.8.cloned.1.call-start = ((), (), s32[]{:S(2)}) async-start(), calls=%async_computation.5 | async-start | bytes 393216 | tf_op jit(solution)/shard_map/psum | solution.py:48
  121.3 33.2 %all-to-all-start.2 = ((bf16[4,1,32]{2,1,0:T(2,128)(2,1)}), bf16[4,1,32]{2,1,0:T(2,128)(2,1)S(1)}, u32[]{:S(2)}, u32[]{:S(2)}) async-start(bf16[4,1,32]{2,1,0:T(2,128)(2,1)} %copy.89), calls=%async_computation.2 | async-start | bytes 4096 | tf_op jit(solution)/shard_map/all_to_all | solution.py:123
  154.6 10.3 %all-to-all-start.1 = ((bf16[4,32,192]{2,1,0:T(8,128)(2,1)}), bf16[4,32,192]{2,1,0:T(8,128)(2,1)S(1)}, u32[]{:S(2)}, u32[]{:S(2)}) async-start(bf16[4,32,192]{2,1,0:T(8,128)(2,1)} %reshape.285), calls=%async_computation.1 | async-start | bytes 131072 | tf_op jit(solution)/shard_map/all_to_all | solution.py:120
Sparse Core Ops, SparseCore 0:
  47.9 30.2 all-reduce.3
  84.0 31.7 all-reduce.5
  120.7 31.6 all-reduce.7
